TPU v7x, 32 devices: a whole 2x2x4 slice. The times are simulated.
32 devices in a mesh: seq: 8 (over y, x, core), fsdp: 4 (over z).
Axes of the slice: x: 2, y: 2, z: 4, core: 2. Of those that a mesh axis runs over, the one named last changes fastest.
Arguments:
- query_states: bfloat16 [2048, 4096], P('seq', 'fsdp'), may hold values from -24 to 24
- key_states: bfloat16 [2048, 4096], P('seq', 'fsdp'), may hold values from -6 to 6
- value_states: bfloat16 [2048, 4096], P('seq', 'fsdp'), may hold values from -6 to 6
- positions: int32 [2048], P('seq'), may hold values from 0 to 2047, as said below
- out_weight: bfloat16 [4096, 5120], P('fsdp', 'seq'), may hold values from -1 to 1
- cotangent: bfloat16 [2048, 5120], P('seq', 'fsdp'), may hold values from -0.59765625 to 0.59765625
Outputs:
- attn_output: float32 [2048, 5120], P('seq', 'fsdp')
- grad_queries: float32 [2048, 4096], P('seq', 'fsdp')
- grad_keys: float32 [2048, 4096], P('seq', 'fsdp')
- grad_values: float32 [2048, 4096], P('seq', 'fsdp')
- grad_weight: float32 [4096, 5120], P('fsdp', 'seq')
Inputs may be any that keep to these rules, and one draw needn't show every extreme that they name: A permutation of 0 to 2047; each aligned block of 256 rows holds, in increasing order, the positions of one residue class modulo 2048 // 256.
All inputs are finite; a program needn't handle non-finite values.
Results may differ from a plain program's by a relative error of at most 0.02.
Values may be sent and summed in bfloat16 or wider, within the bound.
No kernel may reach another device: no remote copies, remote signals or barrier semaphores. Data moves between devices by JAX's collectives and lax.ppermute only.
A program may use at most 128 MiB of HBM per device.

v0:
```python
import jax
import jax.numpy as jnp
from jax import lax
from jax.sharding import PartitionSpec as P

HEAD_DIM = 128
blocked = -1e30


def split_heads(matrix):
    return matrix.reshape(matrix.shape[0], -1, HEAD_DIM)


def masked_scores(query_rows, key_rows, query_pos, key_pos):
    raw = jnp.einsum(
        "qhd,khd->hqk", query_rows, key_rows, preferred_element_type=jnp.float32
    ) * HEAD_DIM ** (-0.5)
    visible = key_pos[None, None, :] <= query_pos[None, :, None]
    return jnp.where(visible, raw, blocked)


def shards(query_states, key_states, value_states, positions, out_weight, cotangent):
    local_tokens = query_states.shape[0]
    query_heads = split_heads(query_states)
    local_heads = query_heads.shape[1]
    all_keys = lax.all_gather(key_states, "seq", axis=0, tiled=True)
    all_values = lax.all_gather(value_states, "seq", axis=0, tiled=True)
    all_pos = lax.all_gather(positions, "seq", axis=0, tiled=True)
    key_heads = split_heads(all_keys)
    value_heads = split_heads(all_values)
    scores = masked_scores(query_heads, key_heads, positions, all_pos)
    row_max = jnp.max(scores, axis=2)
    log_total = row_max + jnp.log(jnp.sum(jnp.exp(scores - row_max[:, :, None]), axis=2))
    probs = jnp.exp(scores - log_total[:, :, None])
    weights = probs.astype(jnp.bfloat16)
    attended = jnp.einsum("hqk,khd->qhd", weights, value_heads, preferred_element_type=jnp.float32)
    attended_heads = attended.astype(jnp.bfloat16)
    attended_flat = attended_heads.reshape(local_tokens, local_heads * HEAD_DIM)
    weight_full = lax.all_gather(out_weight, "seq", axis=1, tiled=True)
    partial_sum = jnp.dot(attended_flat, weight_full, preferred_element_type=jnp.float32).astype(
        jnp.bfloat16
    )
    attn_output = lax.psum_scatter(partial_sum, "fsdp", scatter_dimension=1, tiled=True).astype(
        jnp.float32
    )
    cotangent_full = lax.all_gather(cotangent, "fsdp", axis=1, tiled=True)
    grad_attended = jnp.einsum(
        "td,hd->th", cotangent_full, weight_full, preferred_element_type=jnp.float32
    ).astype(jnp.bfloat16)
    all_attended = lax.all_gather(attended_flat, "seq", axis=0, tiled=True)
    cotangent_cols = lax.all_to_all(cotangent_full, "seq", 1, 0, tiled=True)
    grad_weight = jnp.einsum(
        "th,td->hd", all_attended, cotangent_cols, preferred_element_type=jnp.float32
    )
    grad_heads = split_heads(grad_attended)
    row_delta = jnp.sum(
        grad_heads.astype(jnp.float32) * attended_heads.astype(jnp.float32), axis=2
    ).T
    grad_probs = jnp.einsum(
        "qhd,khd->hqk", grad_heads, value_heads, preferred_element_type=jnp.float32
    )
    grad_scores = (probs * (grad_probs - row_delta[:, :, None])).astype(jnp.bfloat16)
    query_sum = jnp.einsum(
        "hqk,khd->qhd", grad_scores, key_heads, preferred_element_type=jnp.float32
    )
    key_part = jnp.einsum(
        "hqk,qhd->khd", grad_scores, query_heads, preferred_element_type=jnp.float32
    )
    value_part = jnp.einsum("hqk,qhd->khd", weights, grad_heads, preferred_element_type=jnp.float32)
    key_sum = lax.psum_scatter(key_part, "seq", scatter_dimension=0, tiled=True)
    value_sum = lax.psum_scatter(value_part, "seq", scatter_dimension=0, tiled=True)
    score_scale = HEAD_DIM ** (-0.5)
    grad_queries = (query_sum * score_scale).reshape(local_tokens, local_heads * HEAD_DIM)
    grad_keys = (key_sum * score_scale).reshape(local_tokens, local_heads * HEAD_DIM)
    grad_values = value_sum.reshape(local_tokens, local_heads * HEAD_DIM)
    return (attn_output, grad_queries, grad_keys, grad_values, grad_weight)


def solution(mesh):
    in_specs = (
        P("seq", "fsdp"),
        P("seq", "fsdp"),
        P("seq", "fsdp"),
        P("seq"),
        P("fsdp", "seq"),
        P("seq", "fsdp"),
    )
    out_specs = (
        P("seq", "fsdp"),
        P("seq", "fsdp"),
        P("seq", "fsdp"),
        P("seq", "fsdp"),
        P("fsdp", "seq"),
    )
    return jax.shard_map(shards, mesh=mesh, in_specs=in_specs, out_specs=out_specs, check_vma=False)
```

profile of v0, /device:TPU:0, one launch (start us, length us, event | category | flops | bytes accessed | tf_op | source)
XLA Modules:
  0.0 487.9 jit_solution(822385104639132643)
XLA Ops:
  7.2 0.0 copy-start
  7.2 0.0 all-gather.9.cloned.1.call-start
  7.2 0.7 all-gather.9.cloned.1.call-update
  7.9 0.0 all-gather.7.cloned.1.call-start
  8.0 2.0 copy.49
  10.0 0.0 all-gather.7.cloned.1.call-update
  10.0 0.0 all-gather.13.cloned.1.call-start
  10.1 2.2 copy.53
  12.2 0.0 all-gather.13.cloned.1.call-update
  12.3 0.0 all-gather.11.cloned.1.call-start
  12.3 0.5 all-gather.11.cloned.1.call-update
  12.8 0.0 reduce-scatter.4.cloned.1.call-start
  12.9 10.6 %all-gather = s32[8,1,256]{2,1,0:T(1,128)S(1)} all-gather(s32[1,1,256]{2,1,0:T(1,128)} %bitcast.66), channel_id=1, replica_groups=mesh['seq'=8,'fsdp'=4] {'seq'}, dimensions={0}, use_global_device_ids=true | all-gather | bytes 9216 | tf_op jit(solution)/shard_map/all_gather | solution.py:28
  23.5 1.0 broadcast_compare_fusion
  24.5 24.7 %all-gather.9.cloned.1.call-done = bf16[2048,1024]{1,0:T(8,128)(2,1)} async-done(((bf16[256,1024]{1,0:T(8,128)(2,1)}), bf16[2048,1024]{1,0:T(8,128)(2,1)}) %all-gather.9.cloned.1.call-update) | async-done | bytes 4194320 | tf_op jit(solution)/shard_map/all_gather | solution.py:27
  49.2 6.5 %copy.52 = bf16[2048,1024]{0,1:T(8,128)(2,1)} copy(bf16[2048,1024]{1,0:T(8,128)(2,1)} %all-gather.9.cloned.1.call-done) | data formatting | bytes 8388608 | tf_op jit(solution)/shard_map/all_gather | solution.py:27
  55.8 33.3 %all-gather.7.cloned.1.call-done = bf16[2048,1024]{0,1:T(8,128)(2,1)} async-done(((bf16[256,1024]{0,1:T(8,128)(2,1)}), bf16[2048,1024]{0,1:T(8,128)(2,1)}) %all-gather.7.cloned.1.call-update) | async-done | bytes 4194320 | tf_op jit(solution)/shard_map/all_gather | solution.py:26
  89.0 0.0 copy-done
  89.0 5.3 %fusion.1 = (f32[8,256]{1,0:T(8,128)S(1)}, f32[8,256,2048]{2,1,0:T(8,128)S(1)}) fusion(pred[256,2048]{1,0:T(8,128)(4,1)S(1)} %broadcast_compare_fusion, bf16[2048,8,128]{0,2,1:T(8,128)(2,1)} %bitcast.51, bf16[256,1024]{1,0:T(8,128)(2,1)S(1)} %copy-done), kind=kOutput, calls=%fused_computation.5 | convolution fusion | flops 1086322688 | bytes 22028288 | tf_op jit(solution)/shard_map/qhd,khd->hqk/dot_general | solution.py:15
  94.3 0.0 copy-start.1
  94.3 4.5 exponential_reduce_fusion
  98.8 1.7 copy-done.1
  100.5 45.4 %all-gather.13.cloned.1.call-done = bf16[256,5120]{0,1:T(8,128)(2,1)} async-done(((bf16[256,1280]{0,1:T(8,128)(2,1)}), bf16[256,5120]{0,1:T(8,128)(2,1)}) %all-gather.13.cloned.1.call-update) | async-done | bytes 2621456 | tf_op jit(solution)/shard_map/all_gather | solution.py:46
  146.0 63.5 %all-gather.11.cloned.1.call-done = bf16[1024,5120]{1,0:T(8,128)(2,1)} async-done(((bf16[1024,640]{1,0:T(8,128)(2,1)}), bf16[1024,5120]{1,0:T(8,128)(2,1)}) %all-gather.11.cloned.1.call-update) | async-done | bytes 10485776 | tf_op jit(solution)/shard_map/all_gather | solution.py:39
  209.5 7.7 %convolution_convert_fusion.1 = bf16[256,1024]{1,0:T(8,128)(2,1)S(1)} fusion(bf16[256,5120]{0,1:T(8,128)(2,1)} %all-gather.13.cloned.1.call-done, bf16[1024,5120]{1,0:T(8,128)(2,1)} %all-gather.11.cloned.1.call-done), kind=kOutput, calls=%fused_computation.10 | convolution fusion | flops 2684616704 | bytes 13631488 | tf_op jit(solution)/shard_map/td,hd->th/dot_general | solution.py:47
  217.2 0.2 copy.54
  217.4 9.7 %multiply_reduce_fusion = (f32[256,8]{0,1:T(8,128)S(1)}, bf16[8,256,128]{1,2,0:T(8,128)(2,1)S(1)}) fusion(bf16[256,1024]{0,1:T(8,128)(2,1)S(1)} %copy.54, bf16[2048,8,128]{0,2,1:T(8,128)(2,1)} %bitcast.54, f32[8,256,2048]{2,1,0:T(8,128)} %copy-done.1, f32[8,256]{1,0:T(8,128)S(1)} %log_add_fusion, pred[256,2048]{1,0:T(8,128)(4,1)S(1)} %broadcast_compare_fusion), kind=kOutput, calls=%fused_computation.12 | convolution fusion | flops 1091827712 | bytes 22560768 | tf_op jit(solution)/shard_map/hqk,khd->qhd/dot_general | solution.py:36
  227.1 0.0 copy-start.3
  227.1 8.4 %convolution_convert_fusion = bf16[256,5120]{1,0:T(8,128)(2,1)} fusion(bf16[256,1024]{0,1:T(8,128)(2,1)S(1)} %bitcast.57, bf16[1024,5120]{1,0:T(8,128)(2,1)} %all-gather.11.cloned.1.call-done), kind=kOutput, calls=%fused_computation.6 | convolution fusion | flops 2685665280 | bytes 13631488 | tf_op jit(solution)/shard_map/dot_general | solution.py:40
  235.5 0.0 reduce-scatter.4.cloned.1.call-update
  235.6 0.0 copy-done.3
  235.6 0.0 all-gather.15.cloned.1.call-start
  235.6 0.5 all-gather.15.cloned.1.call-update
  236.1 0.2 reduce-scatter.6.cloned.1.call-start
  236.4 11.1 %multiply_convert_fusion = bf16[8,256,2048]{2,1,0:T(8,128)(2,1)S(1)} fusion(f32[8,256,2048]{2,1,0:T(8,128)} %copy-done.1, f32[8,256]{1,0:T(8,128)S(1)} %bitcast.67, f32[8,256]{1,0:T(8,128)S(1)} %log_add_fusion, pred[256,2048]{1,0:T(8,128)(4,1)S(1)} %broadcast_compare_fusion, bf16[256,8,128]{0,2,1:T(8,128)(2,1)S(1)} %bitcast.61, bf16[2048,8,128]{0,2,1:T(8,128)(2,1)} %bitcast.55), kind=kOutput, calls=%fused_computation | convolution fusion | flops 1098907648 | bytes 30425088 | tf_op jit(solution)/shard_map/qhd,khd->hqk/dot_general | solution.py:59
  247.5 0.0 copy-start.2
  247.5 3.2 copy-done.2
  250.7 6.0 %convolution_bitcast_fusion.1 = f32[2048,8,128]{2,0,1:T(8,128)} fusion(bf16[8,256,2048]{2,1,0:T(8,128)(2,1)S(1)} %multiply_convert_fusion, bf16[256,1024]{1,0:T(8,128)(2,1)S(1)} %copy-done), kind=kOutput, calls=%fused_computation.8 | convolution fusion | flops 1073741824 | bytes 17301504 | tf_op jit(solution)/shard_map/hqk,qhd->khd/dot_general | solution.py:66
  256.7 0.0 reduce-scatter.6.cloned.1.call-update
  256.7 0.0 reduce-scatter.8.cloned.1.call-start
  256.8 10.3 %convolution_bitcast_fusion = f32[2048,8,128]{0,2,1:T(8,128)} fusion(bf16[256,8,128]{0,2,1:T(8,128)(2,1)S(1)} %bitcast.62, f32[8,256,2048]{2,1,0:T(8,128)} %copy-done.1, f32[8,256]{1,0:T(8,128)S(1)} %log_add_fusion, pred[256,2048]{1,0:T(8,128)(4,1)S(1)} %broadcast_compare_fusion), kind=kOutput, calls=%fused_computation.7 | convolution fusion | flops 1090519040 | bytes 26222592 | tf_op jit(solution)/shard_map/hqk,qhd->khd/dot_general | solution.py:69
  267.0 0.0 reduce-scatter.8.cloned.1.call-update
  267.0 38.1 %all_to_all.19 = bf16[256,8,640]{0,2,1:T(8,128)(2,1)S(1)} all-to-all(bf16[256,8,640]{0,2,1:T(8,128)(2,1)} %bitcast.59), channel_id=1, replica_groups=mesh['seq'=8,'fsdp'=4] {'seq'}, dimensions={1} | all-to-all | bytes 5242880 | tf_op jit(solution)/shard_map/all_to_all | solution.py:51
  305.1 2.6 copy.60
  307.7 0.0 copy-start.4
  307.7 8.6 %convolution_multiply_fusion = f32[8,256,128]{1,2,0:T(8,128)} fusion(bf16[8,256,2048]{2,1,0:T(8,128)(2,1)} %copy-done.2, bf16[2048,8,128]{0,2,1:T(8,128)(2,1)} %bitcast.52), kind=kOutput, calls=%fused_computation.9 | convolution fusion | flops 1074003968 | bytes 13631488 | tf_op jit(solution)/shard_map/hqk,khd->qhd/dot_general | solution.py:63
  316.3 2.5 copy.61
  318.9 0.0 reduce-scatter.4.cloned.1.call-done
  318.9 2.2 convert_element_type.31
  321.1 7.7 %all-gather.15.cloned.1.call-done = bf16[2048,1024]{0,1:T(8,128)(2,1)} async-done(((bf16[256,1024]{0,1:T(8,128)(2,1)}), bf16[2048,1024]{0,1:T(8,128)(2,1)}) %all-gather.15.cloned.1.call-update) | async-done | bytes 4194320 | tf_op jit(solution)/shard_map/all_gather | solution.py:50
  328.8 0.0 copy-done.4
  328.8 7.1 %fusion.9 = f32[1024,640]{1,0:T(8,128)} fusion(bf16[2048,1024]{0,1:T(8,128)(2,1)} %all-gather.15.cloned.1.call-done, bf16[2048,640]{1,0:T(8,128)(2,1)S(1)} %bitcast.60), kind=kOutput, calls=%fused_computation.21 | convolution fusion | flops 2684354560 | bytes 9437184 | tf_op jit(solution)/shard_map/th,td->hd/dot_general | solution.py:52
  335.9 67.8 %reduce-scatter.6.cloned.1.call-done = f32[256,8,128]{2,0,1:T(8,128)} async-done(((f32[2048,8,128]{2,0,1:T(8,128)}), f32[256,8,128]{2,0,1:T(8,128)}) %reduce-scatter.6.cloned.1.call-update) | async-done | bytes 1048592 | tf_op jit(solution)/shard_map/reduce_scatter | solution.py:70
  403.7 1.3 broadcast_multiply_fusion
  405.0 0.3 copy.59
  405.4 1.3 copy.62
  406.7 71.8 %reduce-scatter.8.cloned.1.call-done = f32[256,8,128]{0,2,1:T(8,128)} async-done(((f32[2048,8,128]{0,2,1:T(8,128)}), f32[256,8,128]{0,2,1:T(8,128)}) %reduce-scatter.8.cloned.1.call-update) | async-done | bytes 1048592 | tf_op jit(solution)/shard_map/reduce_scatter | solution.py:71
  478.5 2.5 copy.63
  (1 shorter events, 0.0 us)
Async XLA Ops:
  7.2 81.9 %copy-start = (bf16[256,1024]{1,0:T(8,128)(2,1)S(1)}, bf16[256,1024]{1,0:T(8,128)(2,1)}, u32[]{:S(2)}) copy-start(bf16[256,1024]{1,0:T(8,128)(2,1)} %param.6) | copy-start | bytes 1572868
  7.2 42.0 %all-gather.9.cloned.1.call-start = ((), (), s32[]{:S(2)}) async-start(), calls=%async_computation.5 | async-start | bytes 4718592 | tf_op jit(solution)/shard_map/all_gather | solution.py:27
  7.9 81.1 %all-gather.7.cloned.1.call-start = ((), (), s32[]{:S(2)}) async-start(), calls=%async_computation.4 | async-start | bytes 4718592 | tf_op jit(solution)/shard_map/all_gather | solution.py:26
  10.0 135.9 %all-gather.13.cloned.1.call-start = ((), (), s32[]{:S(2)}) async-start(), calls=%async_computation.8 | async-start | bytes 3276800 | tf_op jit(solution)/shard_map/all_gather | solution.py:46
  12.3 197.2 %all-gather.11.cloned.1.call-start = ((), (), s32[]{:S(2)}) async-start(), calls=%async_computation.6 | async-start | bytes 11796480 | tf_op jit(solution)/shard_map/all_gather | solution.py:39
  12.8 306.0 %reduce-scatter.4.cloned.1.call-start = ((), (), s32[]{:S(2)}) async-start(), calls=%async_computation.7 | async-start | bytes 3276800 | tf_op jit(solution)/shard_map/reduce_scatter | solution.py:43
  94.3 6.2 %copy-start.1 = (f32[8,256,2048]{2,1,0:T(8,128)}, f32[8,256,2048]{2,1,0:T(8,128)S(1)}, u32[]{:S(2)}) copy-start(f32[8,256,2048]{2,1,0:T(8,128)S(1)} %get-tuple-element.26) | copy-start | bytes 50331652
  227.1 8.4 %copy-start.3 = (bf16[8,256,128]{1,2,0:T(8,128)(2,1)}, bf16[8,256,128]{1,2,0:T(8,128)(2,1)S(1)}, u32[]{:S(2)}) copy-start(bf16[8,256,128]{1,2,0:T(8,128)(2,1)S(1)} %get-tuple-element.28) | copy-start | bytes 1572868
  235.6 93.2 %all-gather.15.cloned.1.call-start = ((), (), s32[]{:S(2)}) async-start(), calls=%async_computation.11 | async-start | bytes 4718592 | tf_op jit(solution)/shard_map/all_gather | solution.py:50
  236.1 167.6 %reduce-scatter.6.cloned.1.call-start = ((), (), s32[]{:S(2)}) async-start(), calls=%async_computation.9 | async-start | bytes 9437184 | tf_op jit(solution)/shard_map/reduce_scatter | solution.py:70
  247.5 3.2 copy-start.2
  256.7 221.8 %reduce-scatter.8.cloned.1.call-start = ((), (), s32[]{:S(2)}) async-start(), calls=%async_computation.10 | async-start | bytes 9437184 | tf_op jit(solution)/shard_map/reduce_scatter | solution.py:71
  307.7 21.1 %copy-start.4 = (bf16[8,256,640]{2,1,0:T(8,128)(2,1)S(1)}, bf16[8,256,640]{2,1,0:T(8,128)(2,1)}, u32[]{:S(2)}) copy-start(bf16[8,256,640]{2,1,0:T(8,128)(2,1)} %copy.60) | copy-start | bytes 7864324
Sparse Core Ops, SparseCore 0:
  9.9 39.2 all-gather.8
  51.7 37.3 all-gather.6
  91.2 54.7 all-gather.12
  147.7 61.7 all-gather.10
  235.7 52.2 reduce-scatter.3
  290.3 38.4 all-gather.14
  332.3 71.3 reduce-scatter.5
  407.2 71.2 reduce-scatter.7
where the time goes:
time: 489 us; the launch traced here: 488 us
  waiting for transfers between devices  316 us (65%)
  matrix products  74.1 us (15%)
  blocking collectives  48.6 us (10%)
  local copies, waits for them, and re-layouts  25.2 us (5%)
  between operations  14.3 us (3%)
  other arithmetic  9.09 us (2%)
    reduce_scatter x1, waiting for transfers between devices, shards(): lax.psum_scatter(value_part, 'seq', scatter_dimension=0, tiled=True)  71.8 us
    reduce_scatter x1, waiting for transfers between devices, shards(): key_sum = lax.psum_scatter(key_part, 'seq', scatter_dimension=0, tiled=True)  67.8 us
    all_gather x1, waiting for transfers between devices, shards(): weight_full = lax.all_gather(out_weight, 'seq', axis=1, tiled=True)  63.5 us
    all_gather x1, waiting for transfers between devices, shards(): cotangent_full = lax.all_gather(cotangent, 'fsdp', axis=1, tiled=True)  45.4 us
    all_to_all x1, blocking collectives, shards(): cotangent_cols = lax.all_to_all(cotangent_full, 'seq', 1, 0, tiled=True)  38.1 us
    all_gather x1, waiting for transfers between devices, shards(): all_keys = lax.all_gather(key_states, 'seq', axis=0, tiled=True)  33.3 us
    all_gather x1, waiting for transfers between devices, shards(): all_values = lax.all_gather(value_states, 'seq', axis=0, tiled=True)  24.7 us
    unnamed x15, local copies, waits for them, and re-layouts  15.5 us
  transfers between devices with their start and end apart: 8, of which 7 were waited for; matrix products, arithmetic and copies ran while one was open for 15% of the time, Pallas kernels for 0%

commit v1 on v0

--- a/solution.py
+++ b/solution.py
@@ -23,7 +23,23 @@
     local_tokens = query_states.shape[0]
     query_heads = split_heads(query_states)
     local_heads = query_heads.shape[1]
-    all_keys = lax.all_gather(key_states, "seq", axis=0, tiled=True)
+    p_next, f_now, ready = (lax.axis_size("seq"), lax.axis_index("seq"), key_states.shape[0])
+    slots = []
+    t = 0
+    while t < p_next:
+        slots.append((t, (t + 1) % p_next))
+        t += 1
+    left_arr = key_states
+    all_keys = jnp.zeros(
+        (*key_states.shape[:0], p_next * ready, *key_states.shape[1:]), key_states.dtype
+    )
+    q = 0
+    while q < p_next:
+        mid_arr = (f_now - q) % p_next
+        all_keys = lax.dynamic_update_slice_in_dim(all_keys, left_arr, mid_arr * ready, axis=0)
+        if q < p_next - 1:
+            left_arr = lax.ppermute(left_arr, axis_name="seq", perm=slots)
+        q += 1
     all_values = lax.all_gather(value_states, "seq", axis=0, tiled=True)
     all_pos = lax.all_gather(positions, "seq", axis=0, tiled=True)
     key_heads = split_heads(all_keys)

time: 489 us -> 461 us (0.943)
  waiting for transfers between devices: 316 us -> 259 us
  local copies, waits for them, and re-layouts: 25.2 us -> 38 us
  matrix products: 74.1 us -> 83.9 us
    ppermute x0 -> x7, waiting for transfers between devices: none -> 61.6 us  [shards(): left_arr = lax.ppermute(left_arr, axis_name='seq', perm=slots)]
    all_gather x1, waiting for transfers between devices: 45.4 us -> 0.01 us  [shards(): cotangent_full = lax.all_gather(cotangent, 'fsdp', axis=1, tiled=True)]
    all_gather x1 -> x0, waiting for transfers between devices: 33.3 us -> none  [shards(): all_keys = lax.all_gather(key_states, 'seq', axis=0, tiled=True)]
    all_gather x1, waiting for transfers between devices: 24.7 us -> 0.02 us  [shards(): all_values = lax.all_gather(value_states, 'seq', axis=0, tiled=True)]
    all_gather x1, waiting for transfers between devices: 63.5 us -> 49.1 us  [shards(): weight_full = lax.all_gather(out_weight, 'seq', axis=1, tiled=True)]
    dynamic_update_slice x0 -> x8, local copies, waits for them, and re-layouts: none -> 7.05 us  [shards(): lax.dynamic_update_slice_in_dim(all_keys, left_arr, mid_arr * ready, axis=0)]
    ppermute x0 -> x7, local copies, waits for them, and re-layouts: none -> 6.64 us  [shards(): left_arr = lax.ppermute(left_arr, axis_name='seq', perm=slots)]
    dot_general x1, matrix products: 5.27 us -> 11.1 us  [masked_scores(): jnp.einsum('qhd,khd->hqk', query_rows, key_rows, preferred_element_type=j...]
  transfers between devices with their start and end apart: 8 -> 14, of which waited for: 7 -> 10; matrix products, arithmetic and copies ran while one was open for 15% -> 22% of each run, Pallas kernels for 0% -> 0%
where the time goes in v1:
time: 461 us; the launch traced here: 460 us
  waiting for transfers between devices  259 us (56%)
  matrix products  83.9 us (18%)
  blocking collectives  50.3 us (11%)
  local copies, waits for them, and re-layouts  38 us (8%)
  between operations  14.5 us (3%)
  other arithmetic  13.2 us (3%)
    reduce_scatter x1, waiting for transfers between devices, shards(): lax.psum_scatter(value_part, 'seq', scatter_dimension=0, tiled=True)  71.8 us
    reduce_scatter x1, waiting for transfers between devices, shards(): key_sum = lax.psum_scatter(key_part, 'seq', scatter_dimension=0, tiled=True)  66.8 us
    ppermute x7, waiting for transfers between devices, shards(): left_arr = lax.ppermute(left_arr, axis_name='seq', perm=slots)  61.6 us
    all_gather x1, waiting for transfers between devices, shards(): weight_full = lax.all_gather(out_weight, 'seq', axis=1, tiled=True)  49.1 us
    all_to_all x1, blocking collectives, shards(): cotangent_cols = lax.all_to_all(cotangent_full, 'seq', 1, 0, tiled=True)  41.3 us
    dot_general x1, matrix products, shards(): jnp.einsum('hqk,qhd->khd', weights, grad_heads, preferred_element_type=jn...  13.6 us
    unnamed x19, local copies, waits for them, and re-layouts  11.8 us
    dot_general x1, matrix products, shards(): jnp.einsum('qhd,khd->hqk', grad_heads, value_heads, preferred_element_typ...  11.7 us
  transfers between devices with their start and end apart: 14, of which 10 were waited for; matrix products, arithmetic and copies ran while one was open for 22% of the time, Pallas kernels for 0%

profile of v1, /device:TPU:0, one launch (start us, length us, event | category | flops | bytes accessed | tf_op | source)
XLA Modules:
  0.0 459.8 jit_solution(17724602555356251132)
XLA Ops:
  7.2 0.0 all-gather.6.cloned.1.call-start
  7.2 0.7 all-gather.6.cloned.1.call-update
  7.9 0.0 all-gather.10.cloned.1.call-start
  8.0 2.2 copy.92
  10.2 0.0 all-gather.8.cloned.1.call-start
  10.2 0.7 all-gather.8.cloned.1.call-update
  10.9 0.0 reduce-scatter.4.cloned.1.call-start
  10.9 0.5 collective-permute-start
  11.5 9.9 %collective-permute-done = bf16[256,1024]{1,0:T(8,128)(2,1)S(1)} collective-permute-done((bf16[256,1024]{1,0:T(8,128)(2,1)}, bf16[256,1024]{1,0:T(8,128)(2,1)S(1)}, u32[]{:S(2)}, u32[]{:S(2)}) %collective-permute-start) | collective-permute-done | bytes 524320 | tf_op jit(solution)/shard_map/ppermute | solution.py:41
  21.4 13.5 %collective-permute-done.1 = bf16[256,1024]{1,0:T(8,128)(2,1)S(1)} collective-permute-done((bf16[256,1024]{1,0:T(8,128)(2,1)S(1)}, bf16[256,1024]{1,0:T(8,128)(2,1)S(1)}, u32[]{:S(2)}, u32[]{:S(2)}) %collective-permute-start.1) | collective-permute-done | bytes 524320 | tf_op jit(solution)/shard_map/ppermute | solution.py:41
  35.0 20.4 %collective-permute-done.2 = bf16[256,1024]{1,0:T(8,128)(2,1)S(1)} collective-permute-done((bf16[256,1024]{1,0:T(8,128)(2,1)S(1)}, bf16[256,1024]{1,0:T(8,128)(2,1)S(1)}, u32[]{:S(2)}, u32[]{:S(2)}) %collective-permute-start.2) | collective-permute-done | bytes 524320 | tf_op jit(solution)/shard_map/ppermute | solution.py:41
  55.4 9.5 %collective-permute-done.3 = bf16[256,1024]{1,0:T(8,128)(2,1)S(1)} collective-permute-done((bf16[256,1024]{1,0:T(8,128)(2,1)S(1)}, bf16[256,1024]{1,0:T(8,128)(2,1)S(1)}, u32[]{:S(2)}, u32[]{:S(2)}) %collective-permute-start.3) | collective-permute-done | bytes 524320 | tf_op jit(solution)/shard_map/ppermute | solution.py:41
  64.9 1.3 copy.80
  66.4 9.0 %all-gather = s32[8,1,256]{2,1,0:T(1,128)S(1)} all-gather(s32[1,1,256]{2,1,0:T(1,128)} %bitcast.78), channel_id=1, replica_groups=mesh['seq'=8,'fsdp'=4] {'seq'}, dimensions={0}, use_global_device_ids=true | all-gather | bytes 9216 | tf_op jit(solution)/shard_map/all_gather | solution.py:44
  75.3 2.5 broadcast_in_dim.21
  77.8 0.9 constant_dynamic-update-slice_fusion.7
  78.7 0.3 collective-permute-start.5
  79.0 0.4 broadcast_compare_fusion
  79.5 1.3 copy.81
  80.7 0.9 constant_dynamic-update-slice_fusion.6
  81.6 1.2 copy.82
  82.9 5.7 %collective-permute-done.5 = bf16[256,1024]{1,0:T(8,128)(2,1)} collective-permute-done((bf16[256,1024]{1,0:T(8,128)(2,1)}, bf16[256,1024]{1,0:T(8,128)(2,1)}, u32[]{:S(2)}, u32[]{:S(2)}) %collective-permute-start.5) | collective-permute-done | bytes 524320 | tf_op jit(solution)/shard_map/ppermute | solution.py:41
  88.5 0.9 constant_dynamic-update-slice_fusion.5
  89.4 0.2 copy.83
  89.6 0.9 constant_dynamic-update-slice_fusion.4
  90.5 0.2 copy.84
  90.7 0.9 constant_dynamic-update-slice_fusion.3
  91.6 1.2 copy.85
  92.8 0.9 constant_dynamic-update-slice_fusion.2
  93.7 1.2 copy.86
  95.0 0.9 constant_dynamic-update-slice_fusion.1
  95.9 2.5 collective-permute-done.6
  98.4 1.2 copy.87
  99.6 0.9 constant_dynamic-update-slice_fusion
  100.5 11.1 %fusion.1 = (f32[8,256]{1,0:T(8,128)S(1)}, f32[8,2048,256]{2,1,0:T(8,128)}) fusion(pred[256,2048]{0,1:T(8,128)(4,1)S(1)} %broadcast_compare_fusion, bf16[2048,8,128]{0,2,1:T(8,128)(2,1)} %bitcast.2, bf16[256,1024]{1,0:T(8,128)(2,1)S(1)} %copy-done), kind=kOutput, calls=%fused_computation.5 | convolution fusion | flops 1086322688 | bytes 22028288 | tf_op jit(solution)/shard_map/qhd,khd->hqk/dot_general | solution.py:15
  111.5 9.2 %exponential_reduce_fusion = f32[8,256]{1,0:T(8,128)S(1)} fusion(f32[8,2048,256]{2,1,0:T(8,128)} %get-tuple-element.26, f32[8,256]{1,0:T(8,128)S(1)} %get-tuple-element.25, pred[256,2048]{0,1:T(8,128)(4,1)S(1)} %broadcast_compare_fusion), kind=kLoop, calls=%fused_computation.3 | loop fusion | flops 16775168 | bytes 17317888 | tf_op jit(solution)/shard_map/reduce_sum | solution.py:49
  120.8 0.0 all-gather.6.cloned.1.call-done
  120.8 6.8 %copy.90 = bf16[2048,1024]{0,1:T(8,128)(2,1)} copy(bf16[2048,1024]{1,0:T(8,128)(2,1)} %all-gather.6.cloned.1.call-done) | data formatting | bytes 8388608 | tf_op jit(solution)/shard_map/all_gather | solution.py:43
  127.6 49.1 %all-gather.8.cloned.1.call-done = bf16[1024,5120]{1,0:T(8,128)(2,1)} async-done(((bf16[1024,640]{1,0:T(8,128)(2,1)}), bf16[1024,5120]{1,0:T(8,128)(2,1)}) %all-gather.8.cloned.1.call-update) | async-done | bytes 10485776 | tf_op jit(solution)/shard_map/all_gather | solution.py:55
  176.7 7.7 %convolution_convert_fusion.1 = bf16[256,1024]{1,0:T(8,128)(2,1)S(1)} fusion(bf16[256,5120]{0,1:T(8,128)(2,1)} %all-gather.10.cloned.1.call-done, bf16[1024,5120]{1,0:T(8,128)(2,1)} %all-gather.8.cloned.1.call-done), kind=kOutput, calls=%fused_computation.10 | convolution fusion | flops 2684616704 | bytes 13631488 | tf_op jit(solution)/shard_map/td,hd->th/dot_general | solution.py:63
  184.5 0.2 copy.93
  184.7 11.2 %multiply_reduce_fusion = (f32[256,8]{0,1:T(8,128)S(1)}, bf16[8,256,128]{1,2,0:T(8,128)(2,1)S(1)}) fusion(bf16[256,1024]{0,1:T(8,128)(2,1)S(1)} %copy.93, bf16[2048,8,128]{0,2,1:T(8,128)(2,1)} %bitcast.67, f32[8,2048,256]{2,1,0:T(8,128)} %get-tuple-element.26, f32[8,256]{1,0:T(8,128)S(1)} %log_add_fusion, pred[256,2048]{0,1:T(8,128)(4,1)S(1)} %broadcast_compare_fusion), kind=kOutput, calls=%fused_computation.12 | convolution fusion | flops 1091827712 | bytes 22560768 | tf_op jit(solution)/shard_map/hqk,khd->qhd/dot_general | solution.py:52
  195.9 8.4 %convolution_convert_fusion = bf16[256,5120]{1,0:T(8,128)(2,1)} fusion(bf16[256,1024]{0,1:T(8,128)(2,1)S(1)} %bitcast.70, bf16[1024,5120]{1,0:T(8,128)(2,1)} %all-gather.8.cloned.1.call-done), kind=kOutput, calls=%fused_computation.6 | convolution fusion | flops 2685665280 | bytes 13631488 | tf_op jit(solution)/shard_map/dot_general | solution.py:56
  204.3 0.0 all-gather.12.cloned.1.call-start
  204.4 0.5 all-gather.12.cloned.1.call-update
  204.9 0.0 reduce-scatter.6.cloned.1.call-start
  205.0 11.7 %multiply_convert_fusion = bf16[8,256,2048]{1,2,0:T(8,128)(2,1)S(1)} fusion(f32[8,2048,256]{2,1,0:T(8,128)} %get-tuple-element.26, f32[8,256]{1,0:T(8,128)S(1)} %bitcast.79, f32[8,256]{1,0:T(8,128)S(1)} %log_add_fusion, pred[256,2048]{0,1:T(8,128)(4,1)S(1)} %broadcast_compare_fusion, bf16[256,8,128]{0,2,1:T(8,128)(2,1)S(1)} %bitcast.74, ...), kind=kOutput, calls=%fused_computation.1 | convolution fusion | flops 1098907648 | bytes 30425088 | tf_op jit(solution)/shard_map/qhd,khd->hqk/dot_general | solution.py:75
  216.7 3.2 copy-done.2
  219.9 5.6 %convolution_bitcast_fusion.1 = f32[2048,8,128]{2,0,1:T(8,128)} fusion(bf16[8,256,2048]{1,2,0:T(8,128)(2,1)S(1)} %multiply_convert_fusion, bf16[256,1024]{1,0:T(8,128)(2,1)S(1)} %copy-done), kind=kOutput, calls=%fused_computation.8 | convolution fusion | flops 1073741824 | bytes 17301504 | tf_op jit(solution)/shard_map/hqk,qhd->khd/dot_general | solution.py:82
  225.5 0.0 reduce-scatter.8.cloned.1.call-start
  225.5 13.6 %convolution_bitcast_fusion = f32[2048,8,128]{0,2,1:T(8,128)} fusion(bf16[256,8,128]{0,2,1:T(8,128)(2,1)S(1)} %bitcast.75, f32[8,2048,256]{2,1,0:T(8,128)} %get-tuple-element.26, f32[8,256]{1,0:T(8,128)S(1)} %log_add_fusion, pred[256,2048]{0,1:T(8,128)(4,1)S(1)} %broadcast_compare_fusion), kind=kOutput, calls=%fused_computation.7 | convolution fusion | flops 1090519040 | bytes 26222592 | tf_op jit(solution)/shard_map/hqk,qhd->khd/dot_general | solution.py:85
  239.2 41.3 %all_to_all.19 = bf16[256,8,640]{0,2,1:T(8,128)(2,1)S(1)} all-to-all(bf16[256,8,640]{0,2,1:T(8,128)(2,1)} %bitcast.72), channel_id=1, replica_groups=mesh['seq'=8,'fsdp'=4] {'seq'}, dimensions={1} | all-to-all | bytes 5242880 | tf_op jit(solution)/shard_map/all_to_all | solution.py:67
  280.6 2.6 copy.101
  283.1 6.6 %convolution_multiply_fusion = f32[8,128,256]{2,1,0:T(8,128)S(1)} fusion(bf16[2048,8,128]{0,2,1:T(8,128)(2,1)} %bitcast.2, bf16[8,256,2048]{1,2,0:T(8,128)(2,1)} %copy-done.2), kind=kOutput, calls=%fused_computation.9 | convolution fusion | flops 1074003968 | bytes 13631488 | tf_op jit(solution)/shard_map/hqk,khd->qhd/dot_general | solution.py:79
  289.8 1.3 copy.102
  291.1 2.2 convert_element_type.31
  293.3 7.6 %all-gather.12.cloned.1.call-done = bf16[2048,1024]{0,1:T(8,128)(2,1)} async-done(((bf16[256,1024]{0,1:T(8,128)(2,1)}), bf16[2048,1024]{0,1:T(8,128)(2,1)}) %all-gather.12.cloned.1.call-update) | async-done | bytes 4194320 | tf_op jit(solution)/shard_map/all_gather | solution.py:66
  300.9 8.0 %fusion.9 = f32[1024,640]{1,0:T(8,128)} fusion(bf16[2048,1024]{0,1:T(8,128)(2,1)} %all-gather.12.cloned.1.call-done, bf16[2048,640]{1,0:T(8,128)(2,1)} %bitcast.73), kind=kOutput, calls=%fused_computation.29 | convolution fusion | flops 2684354560 | bytes 9437184 | tf_op jit(solution)/shard_map/th,td->hd/dot_general | solution.py:68
  308.9 66.8 %reduce-scatter.6.cloned.1.call-done = f32[256,8,128]{2,0,1:T(8,128)} async-done(((f32[2048,8,128]{2,0,1:T(8,128)}), f32[256,8,128]{2,0,1:T(8,128)}) %reduce-scatter.6.cloned.1.call-update) | async-done | bytes 1048592 | tf_op jit(solution)/shard_map/reduce_scatter | solution.py:86
  375.7 1.3 broadcast_multiply_fusion
  377.0 0.3 copy.99
  377.3 1.3 copy.103
  378.6 71.8 %reduce-scatter.8.cloned.1.call-done = f32[256,8,128]{0,2,1:T(8,128)} async-done(((f32[2048,8,128]{0,2,1:T(8,128)}), f32[256,8,128]{0,2,1:T(8,128)}) %reduce-scatter.8.cloned.1.call-update) | async-done | bytes 1048592 | tf_op jit(solution)/shard_map/reduce_scatter | solution.py:87
  450.5 2.5 copy.104
  (26 shorter events, 0.1 us)
Async XLA Ops:
  7.2 93.3 %copy-start = (bf16[256,1024]{1,0:T(8,128)(2,1)S(1)}, bf16[256,1024]{1,0:T(8,128)(2,1)}, u32[]{:S(2)}) copy-start(bf16[256,1024]{1,0:T(8,128)(2,1)} %param.6) | copy-start | bytes 1572868
  7.2 71.8 %copy-start.6 = (s32[256]{0:T(256)S(1)}, s32[256]{0:T(256)}, u32[]{:S(2)}) copy-start(s32[256]{0:T(256)} %param.9) | copy-start | bytes 3076
  7.2 113.6 %all-gather.6.cloned.1.call-start = ((), (), s32[]{:S(2)}) async-start(), calls=%async_computation.4 | async-start | bytes 4718592 | tf_op jit(solution)/shard_map/all_gather | solution.py:43
  7.9 119.7 %all-gather.10.cloned.1.call-start = ((), (), s32[]{:S(2)}) async-start(), calls=%async_computation.7 | async-start | bytes 3276800 | tf_op jit(solution)/shard_map/all_gather | solution.py:62
  10.2 166.6 %all-gather.8.cloned.1.call-start = ((), (), s32[]{:S(2)}) async-start(), calls=%async_computation.5 | async-start | bytes 11796480 | tf_op jit(solution)/shard_map/all_gather | solution.py:55
  10.9 280.2 %reduce-scatter.4.cloned.1.call-start = ((), (), s32[]{:S(2)}) async-start(), calls=%async_computation.6 | async-start | bytes 3276800 | tf_op jit(solution)/shard_map/reduce_scatter | solution.py:59
  10.9 10.5 %collective-permute-start = (bf16[256,1024]{1,0:T(8,128)(2,1)}, bf16[256,1024]{1,0:T(8,128)(2,1)S(1)}, u32[]{:S(2)}, u32[]{:S(2)}) collective-permute-start(bf16[256,1024]{1,0:T(8,128)(2,1)} %param.7), channel_id=1, source_target_pairs={{0,4},{4,8},{8,12},{12,16},{16,20},{20,24},{24,28},{28,0},{1,5},{5... | collective-permute-start | bytes 1572872 | tf_op jit(solution)/shard_map/ppermute | solution.py:41
  21.4 43.5 %copy-start.4 = (bf16[256,1024]{1,0:T(8,128)(2,1)}, bf16[256,1024]{1,0:T(8,128)(2,1)S(1)}, u32[]{:S(2)}) copy-start(bf16[256,1024]{1,0:T(8,128)(2,1)S(1)} %collective-permute-done) | copy-start | bytes 1572868
  21.4 13.5 %collective-permute-start.1 = (bf16[256,1024]{1,0:T(8,128)(2,1)S(1)}, bf16[256,1024]{1,0:T(8,128)(2,1)S(1)}, u32[]{:S(2)}, u32[]{:S(2)}) collective-permute-start(bf16[256,1024]{1,0:T(8,128)(2,1)S(1)} %collective-permute-done), channel_id=1, source_target_pairs={{0,4},{4,8},{8,12},{12,16},{16,20},{20,24},{24,28},{28,0},{1,5},{5... | collective-permute-start | bytes 1572872 | tf_op jit(solution)/shard_map/ppermute | solution.py:41
  35.0 29.9 %copy-start.5 = (bf16[256,1024]{1,0:T(8,128)(2,1)}, bf16[256,1024]{1,0:T(8,128)(2,1)S(1)}, u32[]{:S(2)}) copy-start(bf16[256,1024]{1,0:T(8,128)(2,1)S(1)} %collective-permute-done.1) | copy-start | bytes 1572868
  35.0 20.4 %collective-permute-start.2 = (bf16[256,1024]{1,0:T(8,128)(2,1)S(1)}, bf16[256,1024]{1,0:T(8,128)(2,1)S(1)}, u32[]{:S(2)}, u32[]{:S(2)}) collective-permute-start(bf16[256,1024]{1,0:T(8,128)(2,1)S(1)} %collective-permute-done.1), channel_id=1, source_target_pairs={{0,4},{4,8},{8,12},{12,16},{16,20},{20,24},{24,28},{28,0},{1,5},{5... | collective-permute-start | bytes 1572872 | tf_op jit(solution)/shard_map/ppermute | solution.py:41
  55.4 9.5 %collective-permute-start.3 = (bf16[256,1024]{1,0:T(8,128)(2,1)S(1)}, bf16[256,1024]{1,0:T(8,128)(2,1)S(1)}, u32[]{:S(2)}, u32[]{:S(2)}) collective-permute-start(bf16[256,1024]{1,0:T(8,128)(2,1)S(1)} %collective-permute-done.2), channel_id=1, source_target_pairs={{0,4},{4,8},{8,12},{12,16},{16,20},{20,24},{24,28},{28,0},{1,5},{5... | collective-permute-start | bytes 1572872 | tf_op jit(solution)/shard_map/ppermute | solution.py:41
  64.9 13.8 %collective-permute-start.4 = (bf16[256,1024]{1,0:T(8,128)(2,1)S(1)}, bf16[256,1024]{1,0:T(8,128)(2,1)}, u32[]{:S(2)}, u32[]{:S(2)}) collective-permute-start(bf16[256,1024]{1,0:T(8,128)(2,1)S(1)} %collective-permute-done.3), channel_id=1, source_target_pairs={{0,4},{4,8},{8,12},{12,16},{16,20},{20,24},{24,28},{28,0},{1,5},{5... | collective-permute-start | bytes 1572872 | tf_op jit(solution)/shard_map/ppermute | solution.py:41
  78.7 9.8 %collective-permute-start.5 = (bf16[256,1024]{1,0:T(8,128)(2,1)}, bf16[256,1024]{1,0:T(8,128)(2,1)}, u32[]{:S(2)}, u32[]{:S(2)}) collective-permute-start(bf16[256,1024]{1,0:T(8,128)(2,1)} %collective-permute-done.4), channel_id=1, source_target_pairs={{0,4},{4,8},{8,12},{12,16},{16,20},{20,24},{24,28},{28,0},{1,5},{5... | collective-permute-start | bytes 1572872 | tf_op jit(solution)/shard_map/ppermute | solution.py:41
  88.5 9.8 %collective-permute-start.6 = (bf16[256,1024]{1,0:T(8,128)(2,1)}, bf16[256,1024]{1,0:T(8,128)(2,1)}, u32[]{:S(2)}, u32[]{:S(2)}) collective-permute-start(bf16[256,1024]{1,0:T(8,128)(2,1)} %collective-permute-done.5), channel_id=1, source_target_pairs={{0,4},{4,8},{8,12},{12,16},{16,20},{20,24},{24,28},{28,0},{1,5},{5... | collective-permute-start | bytes 1572872 | tf_op jit(solution)/shard_map/ppermute | solution.py:41
  195.9 8.4 %copy-start.3 = (bf16[8,256,128]{1,2,0:T(8,128)(2,1)}, bf16[8,256,128]{1,2,0:T(8,128)(2,1)S(1)}, u32[]{:S(2)}) copy-start(bf16[8,256,128]{1,2,0:T(8,128)(2,1)S(1)} %get-tuple-element.28) | copy-start | bytes 1572868
  204.3 96.6 %all-gather.12.cloned.1.call-start = ((), (), s32[]{:S(2)}) async-start(), calls=%async_computation.10 | async-start | bytes 4718592 | tf_op jit(solution)/shard_map/all_gather | solution.py:66
  204.9 170.7 %reduce-scatter.6.cloned.1.call-start = ((), (), s32[]{:S(2)}) async-start(), calls=%async_computation.8 | async-start | bytes 9437184 | tf_op jit(solution)/shard_map/reduce_scatter | solution.py:86
  216.7 3.2 copy-start.2
  225.5 225.0 %reduce-scatter.8.cloned.1.call-start = ((), (), s32[]{:S(2)}) async-start(), calls=%async_computation.9 | async-start | bytes 9437184 | tf_op jit(solution)/shard_map/reduce_scatter | solution.py:87
  300.9 152.0 %copy-start.1 = (bf16[256,1024]{1,0:T(8,128)(2,1)S(1)}, bf16[256,1024]{1,0:T(8,128)(2,1)}, u32[]{:S(2)}) copy-start(bf16[256,1024]{1,0:T(8,128)(2,1)} %param.6) | copy-start | bytes 1572868
Sparse Core Ops, SparseCore 0:
  9.9 46.1 all-gather.5
  58.2 54.8 all-gather.9
  114.9 61.7 all-gather.7
  204.4 52.2 reduce-scatter.3
  259.0 41.8 all-gather.11
  304.3 71.3 reduce-scatter.5
  379.1 71.2 reduce-scatter.7
